TPU v7x, 512 devices: a whole 4x8x8 slice. The times are simulated.
512 devices in a mesh: chain: 64 (over y, z), cross: 8 (over x, core).
Axes of the slice: x: 4, y: 8, z: 8, core: 2. Of those that a mesh axis runs over, the one named last changes fastest.
Arguments:
- right_side: bfloat16 [64, 1024, 512], P('chain', 'cross'), may hold values from -6 to 6
- self_factor: bfloat16 [6, 64, 1024, 1024], P(None, 'chain', 'cross')
- lower_factor: bfloat16 [6, 64, 1024, 1024], P(None, 'chain', 'cross'), may hold values from -0.078125 to 0.078125
- upper_factor: bfloat16 [6, 64, 1024, 1024], P(None, 'chain', 'cross'), may hold values from -0.078125 to 0.078125
Outputs:
- solution: bfloat16 [64, 1024, 512], P('chain', 'cross')
All inputs are finite; a program needn't handle non-finite values.
Results may differ from a plain program's by a relative error of at most 0.014.
Values may be sent and summed in bfloat16 or wider, within the bound.
No kernel may reach another device: no remote copies, remote signals or barrier semaphores. Data moves between devices by JAX's collectives and lax.ppermute only.
A program may use at most 64 MiB of HBM per device.

v0:
```python
import jax
import jax.numpy as jnp
from jax import lax
from jax.sharding import PartitionSpec as P


def shifted(value, axis, steps):
    count = lax.axis_size(axis)
    initial, last = (max(0, -steps), min(count, count - steps))
    return lax.ppermute(value, axis, [(source, source + steps) for source in range(initial, last)])


def reach_full(piece, dist):
    lower = shifted(piece, "chain", dist)
    upper = shifted(piece, "chain", -dist)
    return (lower, upper)


def body(right_side, self_factor, lower_factor, upper_factor):
    levels = lax.axis_size("chain").bit_length() - 1
    current = right_side[0]
    for level in range(levels):
        dist = 2**level
        own_mat = self_factor[level, 0]
        low_mat = lower_factor[level, 0]
        up_mat = upper_factor[level, 0]
        whole = lax.all_gather(current, "cross", axis=0, tiled=True)
        lower, upper = reach_full(whole, dist)
        total = jnp.dot(own_mat, whole, preferred_element_type=jnp.float32)
        total = total - jnp.dot(low_mat, lower, preferred_element_type=jnp.float32)
        total = total - jnp.dot(up_mat, upper, preferred_element_type=jnp.float32)
        current = total.astype(jnp.bfloat16)
    return current[None]


def solution(mesh):
    return jax.shard_map(
        body,
        mesh=mesh,
        in_specs=(
            P("chain", "cross", None),
            P(None, "chain", "cross", None),
            P(None, "chain", "cross", None),
            P(None, "chain", "cross", None),
        ),
        out_specs=P("chain", "cross", None),
        check_vma=False,
    )
```

profile of v0, /device:TPU:1, one launch (start us, length us, event | category | flops | bytes accessed | tf_op | source)
XLA Modules:
  0.0 539.7 jit_solution(4165311589859038631)
XLA Ops:
  7.3 37.0 %all-gather.18.cloned.1.call-done = bf16[1,1024,512]{2,1,0:T(8,128)(2,1)} async-done(((bf16[1,128,512]{2,1,0:T(8,128)(2,1)}), bf16[1,1024,512]{2,1,0:T(8,128)(2,1)}) %all-gather.18.cloned.1.call-update) | async-done | bytes 1048592 | tf_op jit(solution)/shard_map/all_gather | solution.py:27
  44.3 3.2 collective-permute-start
  50.4 19.6 %collective-permute-done = bf16[1024,512]{1,0:T(8,128)(2,1)S(1)} collective-permute-done((bf16[1024,512]{1,0:T(8,128)(2,1)}, bf16[1024,512]{1,0:T(8,128)(2,1)S(1)}, u32[]{:S(2)}, u32[]{:S(2)}) %collective-permute-start) | collective-permute-done | bytes 1048608 | tf_op jit(solution)/shard_map/ppermute | solution.py:10
  70.3 3.4 collective-permute-done.1
  75.8 30.0 %all-gather.8.cloned.1.call-done = bf16[1024,512]{1,0:T(8,128)(2,1)} async-done(((bf16[128,512]{1,0:T(8,128)(2,1)}), bf16[1024,512]{1,0:T(8,128)(2,1)}) %all-gather.8.cloned.1.call-update) | async-done | bytes 1048592 | tf_op jit(solution)/shard_map/all_gather | solution.py:27
  105.8 4.2 collective-permute-start.2
  113.1 19.6 %collective-permute-done.2 = bf16[1024,512]{1,0:T(8,128)(2,1)S(1)} collective-permute-done((bf16[1024,512]{1,0:T(8,128)(2,1)}, bf16[1024,512]{1,0:T(8,128)(2,1)S(1)}, u32[]{:S(2)}, u32[]{:S(2)}) %collective-permute-start.2) | collective-permute-done | bytes 1048608 | tf_op jit(solution)/shard_map/ppermute | solution.py:10
  133.1 30.1 %collective-permute-done.3 = bf16[1024,512]{1,0:T(8,128)(2,1)S(1)} collective-permute-done((bf16[1024,512]{1,0:T(8,128)(2,1)}, bf16[1024,512]{1,0:T(8,128)(2,1)S(1)}, u32[]{:S(2)}, u32[]{:S(2)}) %collective-permute-start.3) | collective-permute-done | bytes 1048608 | tf_op jit(solution)/shard_map/ppermute | solution.py:10
  163.2 2.1 fusion.10
  165.4 25.3 %all-gather.10.cloned.1.call-done = bf16[1024,512]{0,1:T(8,128)(2,1)} async-done(((bf16[128,512]{0,1:T(8,128)(2,1)}), bf16[1024,512]{0,1:T(8,128)(2,1)}) %all-gather.10.cloned.1.call-update) | async-done | bytes 1048592 | tf_op jit(solution)/shard_map/all_gather | solution.py:27
  190.7 7.8 %collective-permute-start.4 = (bf16[1024,512]{0,1:T(8,128)(2,1)}, bf16[1024,512]{0,1:T(8,128)(2,1)S(1)}, u32[]{:S(2)}, u32[]{:S(2)}) collective-permute-start(bf16[1024,512]{0,1:T(8,128)(2,1)} %all-gather.10.cloned.1.call-done), channel_id=1, source_target_pairs={{0,32},{8,40},{16,48},{24,56},{32,64},{40,72},{48,80},{56,88},{64,... | collective-permute-start | bytes 3145736 | tf_op jit(solution)/shard_map/ppermute | solution.py:10
  201.4 65.5 %collective-permute-done.4 = bf16[1024,512]{0,1:T(8,128)(2,1)S(1)} collective-permute-done((bf16[1024,512]{0,1:T(8,128)(2,1)}, bf16[1024,512]{0,1:T(8,128)(2,1)S(1)}, u32[]{:S(2)}, u32[]{:S(2)}) %collective-permute-start.4) | collective-permute-done | bytes 1048608 | tf_op jit(solution)/shard_map/ppermute | solution.py:10
  269.5 54.1 %all-gather.12.cloned.1.call-done = bf16[1024,512]{0,1:T(8,128)(2,1)} async-done(((bf16[128,512]{0,1:T(8,128)(2,1)}), bf16[1024,512]{0,1:T(8,128)(2,1)}) %all-gather.12.cloned.1.call-update) | async-done | bytes 1048592 | tf_op jit(solution)/shard_map/all_gather | solution.py:27
  323.7 3.2 collective-permute-start.6
  329.8 19.5 %collective-permute-done.6 = bf16[1024,512]{0,1:T(8,128)(2,1)S(1)} collective-permute-done((bf16[1024,512]{0,1:T(8,128)(2,1)}, bf16[1024,512]{0,1:T(8,128)(2,1)S(1)}, u32[]{:S(2)}, u32[]{:S(2)}) %collective-permute-start.6) | collective-permute-done | bytes 1048608 | tf_op jit(solution)/shard_map/ppermute | solution.py:10
  349.8 3.3 collective-permute-done.7
  355.2 31.2 %all-gather.14.cloned.1.call-done = bf16[1024,512]{0,1:T(8,128)(2,1)} async-done(((bf16[128,512]{0,1:T(8,128)(2,1)}), bf16[1024,512]{0,1:T(8,128)(2,1)}) %all-gather.14.cloned.1.call-update) | async-done | bytes 1048592 | tf_op jit(solution)/shard_map/all_gather | solution.py:27
  386.4 4.1 collective-permute-start.8
  393.5 19.6 %collective-permute-done.8 = bf16[1024,512]{0,1:T(8,128)(2,1)S(1)} collective-permute-done((bf16[1024,512]{0,1:T(8,128)(2,1)}, bf16[1024,512]{0,1:T(8,128)(2,1)S(1)}, u32[]{:S(2)}, u32[]{:S(2)}) %collective-permute-start.8) | collective-permute-done | bytes 1048608 | tf_op jit(solution)/shard_map/ppermute | solution.py:10
  413.5 28.4 %collective-permute-done.9 = bf16[1024,512]{0,1:T(8,128)(2,1)S(1)} collective-permute-done((bf16[1024,512]{0,1:T(8,128)(2,1)}, bf16[1024,512]{0,1:T(8,128)(2,1)S(1)}, u32[]{:S(2)}, u32[]{:S(2)}) %collective-permute-start.9) | collective-permute-done | bytes 1048608 | tf_op jit(solution)/shard_map/ppermute | solution.py:10
  444.0 28.5 %all-gather.16.cloned.1.call-done = bf16[1024,512]{0,1:T(8,128)(2,1)} async-done(((bf16[128,512]{0,1:T(8,128)(2,1)}), bf16[1024,512]{0,1:T(8,128)(2,1)}) %all-gather.16.cloned.1.call-update) | async-done | bytes 1048592 | tf_op jit(solution)/shard_map/all_gather | solution.py:27
  472.5 7.1 %collective-permute-start.10 = (bf16[1024,512]{0,1:T(8,128)(2,1)}, bf16[1024,512]{0,1:T(8,128)(2,1)S(1)}, u32[]{:S(2)}, u32[]{:S(2)}) collective-permute-start(bf16[1024,512]{0,1:T(8,128)(2,1)} %all-gather.16.cloned.1.call-done), channel_id=1, source_target_pairs={{0,256},{8,264},{16,272},{24,280},{32,288},{40,296},{48,304},{56,3... | collective-permute-start | bytes 3145736 | tf_op jit(solution)/shard_map/ppermute | solution.py:10
  482.6 32.1 %collective-permute-done.10 = bf16[1024,512]{0,1:T(8,128)(2,1)S(1)} collective-permute-done((bf16[1024,512]{0,1:T(8,128)(2,1)}, bf16[1024,512]{0,1:T(8,128)(2,1)S(1)}, u32[]{:S(2)}, u32[]{:S(2)}) %collective-permute-start.10) | collective-permute-done | bytes 1048608 | tf_op jit(solution)/shard_map/ppermute | solution.py:10
  515.1 15.6 %collective-permute-done.11 = bf16[1024,512]{0,1:T(8,128)(2,1)S(1)} collective-permute-done((bf16[1024,512]{0,1:T(8,128)(2,1)}, bf16[1024,512]{0,1:T(8,128)(2,1)S(1)}, u32[]{:S(2)}, u32[]{:S(2)}) %collective-permute-start.11) | collective-permute-done | bytes 1048608 | tf_op jit(solution)/shard_map/ppermute | solution.py:10
  (41 shorter events, 31.5 us)
Async XLA Ops:
  6.5 63.5 %copy-start = (bf16[6,1,128,1024]{3,2,1,0:T(8,128)(2,1)S(1)}, bf16[6,1,128,1024]{3,2,1,0:T(8,128)(2,1)}, u32[]{:S(2)}) copy-start(bf16[6,1,128,1024]{3,2,1,0:T(8,128)(2,1)} %param.6) | copy-start | bytes 4718596
  6.5 37.8 %all-gather.18.cloned.1.call-start = ((), (), s32[]{:S(2)}) async-start(), calls=%async_computation.5 | async-start | bytes 1179648 | tf_op jit(solution)/shard_map/all_gather | solution.py:27
  7.3 98.6 %all-gather.8.cloned.1.call-start = ((), (), s32[]{:S(2)}) async-start(), calls=%async_computation | async-start | bytes 1179648 | tf_op jit(solution)/shard_map/all_gather | solution.py:27
  44.3 25.7 %collective-permute-start = (bf16[1024,512]{1,0:T(8,128)(2,1)}, bf16[1024,512]{1,0:T(8,128)(2,1)S(1)}, u32[]{:S(2)}, u32[]{:S(2)}) collective-permute-start(bf16[1024,512]{1,0:T(8,128)(2,1)} %bitcast.86), channel_id=1, source_target_pairs={{0,8},{8,16},{16,24},{24,32},{32,40},{40,48},{48,56},{56,64},{64,7... | collective-permute-start | bytes 3145736 | tf_op jit(solution)/shard_map/ppermute | solution.py:10
  47.5 26.3 %collective-permute-start.1 = (bf16[1024,512]{1,0:T(8,128)(2,1)}, bf16[1024,512]{1,0:T(8,128)(2,1)S(1)}, u32[]{:S(2)}, u32[]{:S(2)}) collective-permute-start(bf16[1024,512]{1,0:T(8,128)(2,1)} %bitcast.87), channel_id=1, source_target_pairs={{8,0},{16,8},{24,16},{32,24},{40,32},{48,40},{56,48},{64,56},{72,6... | collective-permute-start | bytes 3145736 | tf_op jit(solution)/shard_map/ppermute | solution.py:10
  50.4 61.0 %copy-start.1 = (bf16[6,1,128,1024]{3,2,1,0:T(8,128)(2,1)S(1)}, bf16[6,1,128,1024]{3,2,1,0:T(8,128)(2,1)}, u32[]{:S(2)}) copy-start(bf16[6,1,128,1024]{3,2,1,0:T(8,128)(2,1)} %param.5) | copy-start | bytes 4718596
  75.7 115.0 %all-gather.10.cloned.1.call-start = ((), (), s32[]{:S(2)}) async-start(), calls=%async_computation.1 | async-start | bytes 1179648 | tf_op jit(solution)/shard_map/all_gather | solution.py:27
  105.8 26.8 %collective-permute-start.2 = (bf16[1024,512]{1,0:T(8,128)(2,1)}, bf16[1024,512]{1,0:T(8,128)(2,1)S(1)}, u32[]{:S(2)}, u32[]{:S(2)}) collective-permute-start(bf16[1024,512]{1,0:T(8,128)(2,1)} %all-gather.8.cloned.1.call-done), channel_id=1, source_target_pairs={{0,16},{8,24},{16,32},{24,40},{32,48},{40,56},{48,64},{56,72},{64,... | collective-permute-start | bytes 3145736 | tf_op jit(solution)/shard_map/ppermute | solution.py:10
  110.1 53.2 %collective-permute-start.3 = (bf16[1024,512]{1,0:T(8,128)(2,1)}, bf16[1024,512]{1,0:T(8,128)(2,1)S(1)}, u32[]{:S(2)}, u32[]{:S(2)}) collective-permute-start(bf16[1024,512]{1,0:T(8,128)(2,1)} %all-gather.8.cloned.1.call-done), channel_id=1, source_target_pairs={{16,0},{24,8},{32,16},{40,24},{48,32},{56,40},{64,48},{72,56},{80,... | collective-permute-start | bytes 3145736 | tf_op jit(solution)/shard_map/ppermute | solution.py:10
  165.3 158.3 %all-gather.12.cloned.1.call-start = ((), (), s32[]{:S(2)}) async-start(), calls=%async_computation.2 | async-start | bytes 1179648 | tf_op jit(solution)/shard_map/all_gather | solution.py:27
  190.7 76.3 %collective-permute-start.4 = (bf16[1024,512]{0,1:T(8,128)(2,1)}, bf16[1024,512]{0,1:T(8,128)(2,1)S(1)}, u32[]{:S(2)}, u32[]{:S(2)}) collective-permute-start(bf16[1024,512]{0,1:T(8,128)(2,1)} %all-gather.10.cloned.1.call-done), channel_id=1, source_target_pairs={{0,32},{8,40},{16,48},{24,56},{32,64},{40,72},{48,80},{56,88},{64,... | collective-permute-start | bytes 3145736 | tf_op jit(solution)/shard_map/ppermute | solution.py:10
  198.5 69.0 %collective-permute-start.5 = (bf16[1024,512]{0,1:T(8,128)(2,1)}, bf16[1024,512]{0,1:T(8,128)(2,1)S(1)}, u32[]{:S(2)}, u32[]{:S(2)}) collective-permute-start(bf16[1024,512]{0,1:T(8,128)(2,1)} %all-gather.10.cloned.1.call-done), channel_id=1, source_target_pairs={{32,0},{40,8},{48,16},{56,24},{64,32},{72,40},{80,48},{88,56},{96,... | collective-permute-start | bytes 3145736 | tf_op jit(solution)/shard_map/ppermute | solution.py:10
  269.5 116.9 %all-gather.14.cloned.1.call-start = ((), (), s32[]{:S(2)}) async-start(), calls=%async_computation.3 | async-start | bytes 1179648 | tf_op jit(solution)/shard_map/all_gather | solution.py:27
  323.7 25.7 %collective-permute-start.6 = (bf16[1024,512]{0,1:T(8,128)(2,1)}, bf16[1024,512]{0,1:T(8,128)(2,1)S(1)}, u32[]{:S(2)}, u32[]{:S(2)}) collective-permute-start(bf16[1024,512]{0,1:T(8,128)(2,1)} %all-gather.12.cloned.1.call-done), channel_id=1, source_target_pairs={{0,64},{8,72},{16,80},{24,88},{32,96},{40,104},{48,112},{56,120},{... | collective-permute-start | bytes 3145736 | tf_op jit(solution)/shard_map/ppermute | solution.py:10
  326.8 26.3 %collective-permute-start.7 = (bf16[1024,512]{0,1:T(8,128)(2,1)}, bf16[1024,512]{0,1:T(8,128)(2,1)S(1)}, u32[]{:S(2)}, u32[]{:S(2)}) collective-permute-start(bf16[1024,512]{0,1:T(8,128)(2,1)} %all-gather.12.cloned.1.call-done), channel_id=1, source_target_pairs={{64,0},{72,8},{80,16},{88,24},{96,32},{104,40},{112,48},{120,56},{... | collective-permute-start | bytes 3145736 | tf_op jit(solution)/shard_map/ppermute | solution.py:10
  355.2 117.4 %all-gather.16.cloned.1.call-start = ((), (), s32[]{:S(2)}) async-start(), calls=%async_computation.4 | async-start | bytes 1179648 | tf_op jit(solution)/shard_map/all_gather | solution.py:27
  386.4 26.6 %collective-permute-start.8 = (bf16[1024,512]{0,1:T(8,128)(2,1)}, bf16[1024,512]{0,1:T(8,128)(2,1)S(1)}, u32[]{:S(2)}, u32[]{:S(2)}) collective-permute-start(bf16[1024,512]{0,1:T(8,128)(2,1)} %all-gather.14.cloned.1.call-done), channel_id=1, source_target_pairs={{0,128},{8,136},{16,144},{24,152},{32,160},{40,168},{48,176},{56,1... | collective-permute-start | bytes 3145736 | tf_op jit(solution)/shard_map/ppermute | solution.py:10
  390.5 51.5 %collective-permute-start.9 = (bf16[1024,512]{0,1:T(8,128)(2,1)}, bf16[1024,512]{0,1:T(8,128)(2,1)S(1)}, u32[]{:S(2)}, u32[]{:S(2)}) collective-permute-start(bf16[1024,512]{0,1:T(8,128)(2,1)} %all-gather.14.cloned.1.call-done), channel_id=1, source_target_pairs={{128,0},{136,8},{144,16},{152,24},{160,32},{168,40},{176,48},{184,... | collective-permute-start | bytes 3145736 | tf_op jit(solution)/shard_map/ppermute | solution.py:10
  472.5 42.2 %collective-permute-start.10 = (bf16[1024,512]{0,1:T(8,128)(2,1)}, bf16[1024,512]{0,1:T(8,128)(2,1)S(1)}, u32[]{:S(2)}, u32[]{:S(2)}) collective-permute-start(bf16[1024,512]{0,1:T(8,128)(2,1)} %all-gather.16.cloned.1.call-done), channel_id=1, source_target_pairs={{0,256},{8,264},{16,272},{24,280},{32,288},{40,296},{48,304},{56,3... | collective-permute-start | bytes 3145736 | tf_op jit(solution)/shard_map/ppermute | solution.py:10
  479.7 51.0 %collective-permute-start.11 = (bf16[1024,512]{0,1:T(8,128)(2,1)}, bf16[1024,512]{0,1:T(8,128)(2,1)S(1)}, u32[]{:S(2)}, u32[]{:S(2)}) collective-permute-start(bf16[1024,512]{0,1:T(8,128)(2,1)} %all-gather.16.cloned.1.call-done), channel_id=1, source_target_pairs={{256,0},{264,8},{272,16},{280,24},{288,32},{296,40},{304,48},{312,... | collective-permute-start | bytes 3145736 | tf_op jit(solution)/shard_map/ppermute | solution.py:10
Sparse Core Ops, SparseCore 0:
  9.5 34.7 all-gather.17
  75.8 29.9 all-gather.7
  165.5 25.1 all-gather.9
  269.6 53.9 all-gather.11
  355.3 31.0 all-gather.13
  444.1 28.3 all-gather.15
where the time goes:
time: 540 us
  waiting for transfers between devices  464 us (86%)
  starting transfers between devices  37.5 us (7%)
  matrix products  24.1 us (4%)
  between operations  13.7 us (3%)
    ppermute x12, waiting for transfers between devices, shifted(): lax.ppermute(value, axis, [(source, source + steps) for source in range(i...  257 us
    all_gather x6, waiting for transfers between devices, body(): whole = lax.all_gather(current, 'cross', axis=0, tiled=True)  206 us
    ppermute x12, starting transfers between devices, shifted(): lax.ppermute(value, axis, [(source, source + steps) for source in range(i...  37.3 us
    dot_general x6, matrix products, body(): total = total - jnp.dot(up_mat, upper, preferred_element_type=jnp.float32)  11.5 us
  transfers between devices with their start and end apart: 18, of which 17 were waited for; matrix products, arithmetic and copies ran while one was open for 2% of the time, Pallas kernels for 0%

commit v1 on v0

--- a/solution.py
+++ b/solution.py
@@ -24,7 +24,26 @@
         own_mat = self_factor[level, 0]
         low_mat = lower_factor[level, 0]
         up_mat = upper_factor[level, 0]
-        whole = lax.all_gather(current, "cross", axis=0, tiled=True)
+        devices, mine, rows = (lax.axis_size("cross"), lax.axis_index("cross"), current.shape[0])
+        upward = [(i, (i + 1) % devices) for i in range(devices)]
+        left = [(i, (i - 1) % devices) for i in range(devices)]
+        out = jnp.zeros(
+            (*current.shape[:0], devices * rows, *current.shape[0 + 1 :]), current.dtype
+        )
+        out = lax.dynamic_update_slice_in_dim(out, current, mine * rows, axis=0)
+        from_left = from_right = current
+        half = devices // 2
+        for step in range(1, half + 1):
+            from_left = lax.ppermute(from_left, "cross", upward)
+            out = lax.dynamic_update_slice_in_dim(
+                out, from_left, (mine - step) % devices * rows, axis=0
+            )
+            if step < devices - half:
+                from_right = lax.ppermute(from_right, "cross", left)
+                out = lax.dynamic_update_slice_in_dim(
+                    out, from_right, (mine + step) % devices * rows, axis=0
+                )
+        whole = out
         lower, upper = reach_full(whole, dist)
         total = jnp.dot(own_mat, whole, preferred_element_type=jnp.float32)
         total = total - jnp.dot(low_mat, lower, preferred_element_type=jnp.float32)

time: 540 us -> 448 us (0.83)
  the two profiles are of different devices: /device:TPU:1 before, /device:TPU:32 now
where the time goes in v1:
time: 448 us
  waiting for transfers between devices  336 us (75%)
  starting transfers between devices  98.1 us (22%)
  matrix products  8.2 us (2%)
  local copies, waits for them, and re-layouts  4.99 us (1%)
    ppermute x12, waiting for transfers between devices, shifted(): lax.ppermute(value, axis, [(source, source + steps) for source in range(i...  258 us
    ppermute x24, waiting for transfers between devices, body(): from_left = lax.ppermute(from_left, 'cross', upward)  77.7 us
    ppermute x18, starting transfers between devices, body(): from_right = lax.ppermute(from_right, 'cross', left)  53.2 us
    ppermute x12, starting transfers between devices, shifted(): lax.ppermute(value, axis, [(source, source + steps) for source in range(i...  44.7 us
  transfers between devices with their start and end apart: 54, of which 35 were waited for; matrix products, arithmetic and copies ran while one was open for 1% of the time, Pallas kernels for 0%

profile of v1, /device:TPU:32, one launch (start us, length us, event | category | flops | bytes accessed | tf_op | source)
XLA Modules:
  0.0 448.0 jit_solution(862060390657990457)
XLA Ops:
  17.7 5.4 %collective-permute-done.6 = bf16[128,512]{1,0:T(8,128)(2,1)S(1)} collective-permute-done((bf16[128,512]{1,0:T(8,128)(2,1)S(1)}, bf16[128,512]{1,0:T(8,128)(2,1)S(1)}, u32[]{:S(2)}, u32[]{:S(2)}) %collective-permute-start.6) | collective-permute-done | bytes 131104 | tf_op jit(solution)/shard_map/ppermute | solution.py:37
  23.2 11.0 %collective-permute-start.8 = (bf16[1024,512]{0,1:T(8,128)(2,1)S(1)}, bf16[1024,512]{0,1:T(8,128)(2,1)S(1)}, u32[]{:S(2)}, u32[]{:S(2)}) collective-permute-start(bf16[1024,512]{0,1:T(8,128)(2,1)S(1)} %constant_dynamic-update-slice_fusion.40), channel_id=1, source_target_pairs={{8,0},{16,8},{24,16},{32,24},{40,32},{48,40},{56,48},{64,56},{72,6... | collective-permute-start | bytes 3145736 | tf_op jit(solution)/shard_map/ppermute | solution.py:10
  36.1 16.4 %collective-permute-done.8 = bf16[1024,512]{0,1:T(8,128)(2,1)S(1)} collective-permute-done((bf16[1024,512]{0,1:T(8,128)(2,1)S(1)}, bf16[1024,512]{0,1:T(8,128)(2,1)S(1)}, u32[]{:S(2)}, u32[]{:S(2)}) %collective-permute-start.8) | collective-permute-done | bytes 1048608 | tf_op jit(solution)/shard_map/ppermute | solution.py:10
  53.0 7.0 %collective-permute-done.7 = bf16[1024,512]{0,1:T(8,128)(2,1)S(1)} collective-permute-done((bf16[1024,512]{0,1:T(8,128)(2,1)S(1)}, bf16[1024,512]{0,1:T(8,128)(2,1)S(1)}, u32[]{:S(2)}, u32[]{:S(2)}) %collective-permute-start.7) | collective-permute-done | bytes 1048608 | tf_op jit(solution)/shard_map/ppermute | solution.py:10
  72.3 3.0 collective-permute-start.14
  78.0 5.5 %collective-permute-done.15 = bf16[128,512]{0,1:T(8,128)(2,1)S(1)} collective-permute-done((bf16[128,512]{0,1:T(8,128)(2,1)S(1)}, bf16[128,512]{0,1:T(8,128)(2,1)S(1)}, u32[]{:S(2)}, u32[]{:S(2)}) %collective-permute-start.15) | collective-permute-done | bytes 131104 | tf_op jit(solution)/shard_map/ppermute | solution.py:37
  85.4 4.8 %collective-permute-start.16 = (bf16[1024,512]{0,1:T(8,128)(2,1)S(1)}, bf16[1024,512]{0,1:T(8,128)(2,1)S(1)}, u32[]{:S(2)}, u32[]{:S(2)}) collective-permute-start(bf16[1024,512]{0,1:T(8,128)(2,1)S(1)} %constant_dynamic-update-slice_fusion.32), channel_id=1, source_target_pairs={{0,16},{8,24},{16,32},{24,40},{32,48},{40,56},{48,64},{56,72},{64,... | collective-permute-start | bytes 3145736 | tf_op jit(solution)/shard_map/ppermute | solution.py:10
  90.3 39.5 %collective-permute-done.17 = bf16[1024,512]{0,1:T(8,128)(2,1)S(1)} collective-permute-done((bf16[1024,512]{0,1:T(8,128)(2,1)S(1)}, bf16[1024,512]{0,1:T(8,128)(2,1)S(1)}, u32[]{:S(2)}, u32[]{:S(2)}) %collective-permute-start.17) | collective-permute-done | bytes 1048608 | tf_op jit(solution)/shard_map/ppermute | solution.py:10
  130.2 4.1 collective-permute-done.16
  141.0 3.0 collective-permute-start.21
  146.6 3.0 collective-permute-start.23
  152.3 5.5 %collective-permute-done.24 = bf16[128,512]{0,1:T(8,128)(2,1)S(1)} collective-permute-done((bf16[128,512]{0,1:T(8,128)(2,1)S(1)}, bf16[128,512]{0,1:T(8,128)(2,1)S(1)}, u32[]{:S(2)}, u32[]{:S(2)}) %collective-permute-start.24) | collective-permute-done | bytes 131104 | tf_op jit(solution)/shard_map/ppermute | solution.py:37
  159.7 7.8 %collective-permute-start.25 = (bf16[1024,512]{0,1:T(8,128)(2,1)S(1)}, bf16[1024,512]{0,1:T(8,128)(2,1)S(1)}, u32[]{:S(2)}, u32[]{:S(2)}) collective-permute-start(bf16[1024,512]{0,1:T(8,128)(2,1)S(1)} %constant_dynamic-update-slice_fusion.24), channel_id=1, source_target_pairs={{0,32},{8,40},{16,48},{24,56},{32,64},{40,72},{48,80},{56,88},{64,... | collective-permute-start | bytes 3145736 | tf_op jit(solution)/shard_map/ppermute | solution.py:10
  167.6 82.4 %collective-permute-done.26 = bf16[1024,512]{0,1:T(8,128)(2,1)S(1)} collective-permute-done((bf16[1024,512]{0,1:T(8,128)(2,1)S(1)}, bf16[1024,512]{0,1:T(8,128)(2,1)S(1)}, u32[]{:S(2)}, u32[]{:S(2)}) %collective-permute-start.26) | collective-permute-done | bytes 1048608 | tf_op jit(solution)/shard_map/ppermute | solution.py:10
  257.1 3.0 collective-permute-start.30
  268.4 5.5 %collective-permute-done.33 = bf16[128,512]{0,1:T(8,128)(2,1)S(1)} collective-permute-done((bf16[128,512]{0,1:T(8,128)(2,1)S(1)}, bf16[128,512]{0,1:T(8,128)(2,1)S(1)}, u32[]{:S(2)}, u32[]{:S(2)}) %collective-permute-start.33) | collective-permute-done | bytes 131104 | tf_op jit(solution)/shard_map/ppermute | solution.py:37
  275.9 3.9 collective-permute-start.34
  279.8 16.8 %collective-permute-done.35 = bf16[1024,512]{0,1:T(8,128)(2,1)S(1)} collective-permute-done((bf16[1024,512]{0,1:T(8,128)(2,1)S(1)}, bf16[1024,512]{0,1:T(8,128)(2,1)S(1)}, u32[]{:S(2)}, u32[]{:S(2)}) %collective-permute-start.35) | collective-permute-done | bytes 1048608 | tf_op jit(solution)/shard_map/ppermute | solution.py:10
  317.8 5.5 %collective-permute-done.42 = bf16[128,512]{0,1:T(8,128)(2,1)S(1)} collective-permute-done((bf16[128,512]{0,1:T(8,128)(2,1)S(1)}, bf16[128,512]{0,1:T(8,128)(2,1)S(1)}, u32[]{:S(2)}, u32[]{:S(2)}) %collective-permute-start.42) | collective-permute-done | bytes 131104 | tf_op jit(solution)/shard_map/ppermute | solution.py:37
  325.3 4.9 %collective-permute-start.43 = (bf16[1024,512]{0,1:T(8,128)(2,1)S(1)}, bf16[1024,512]{0,1:T(8,128)(2,1)S(1)}, u32[]{:S(2)}, u32[]{:S(2)}) collective-permute-start(bf16[1024,512]{0,1:T(8,128)(2,1)S(1)} %constant_dynamic-update-slice_fusion.8), channel_id=1, source_target_pairs={{0,128},{8,136},{16,144},{24,152},{32,160},{40,168},{48,176},{56,1... | collective-permute-start | bytes 3145736 | tf_op jit(solution)/shard_map/ppermute | solution.py:10
  330.1 39.2 %collective-permute-done.44 = bf16[1024,512]{0,1:T(8,128)(2,1)S(1)} collective-permute-done((bf16[1024,512]{0,1:T(8,128)(2,1)S(1)}, bf16[1024,512]{0,1:T(8,128)(2,1)S(1)}, u32[]{:S(2)}, u32[]{:S(2)}) %collective-permute-start.44) | collective-permute-done | bytes 1048608 | tf_op jit(solution)/shard_map/ppermute | solution.py:10
  390.5 5.5 %collective-permute-done.51 = bf16[128,512]{0,1:T(8,128)(2,1)S(1)} collective-permute-done((bf16[128,512]{0,1:T(8,128)(2,1)S(1)}, bf16[128,512]{0,1:T(8,128)(2,1)S(1)}, u32[]{:S(2)}, u32[]{:S(2)}) %collective-permute-start.51) | collective-permute-done | bytes 131104 | tf_op jit(solution)/shard_map/ppermute | solution.py:37
  398.7 17.8 %collective-permute-done.53 = bf16[1024,512]{0,1:T(8,128)(2,1)S(1)} collective-permute-done((bf16[1024,512]{0,1:T(8,128)(2,1)S(1)}, bf16[1024,512]{0,1:T(8,128)(2,1)S(1)}, u32[]{:S(2)}, u32[]{:S(2)}) %collective-permute-start.53) | collective-permute-done | bytes 1048608 | tf_op jit(solution)/shard_map/ppermute | solution.py:10
  416.9 29.4 %collective-permute-done.52 = bf16[1024,512]{0,1:T(8,128)(2,1)S(1)} collective-permute-done((bf16[1024,512]{0,1:T(8,128)(2,1)S(1)}, bf16[1024,512]{0,1:T(8,128)(2,1)S(1)}, u32[]{:S(2)}, u32[]{:S(2)}) %collective-permute-start.52) | collective-permute-done | bytes 1048608 | tf_op jit(solution)/shard_map/ppermute | solution.py:10
  (166 shorter events, 117.3 us)
Async XLA Ops:
  0.0 5.8 %collective-permute-start = (bf16[128,512]{1,0:T(8,128)(2,1)}, bf16[128,512]{1,0:T(8,128)(2,1)S(1)}, u32[]{:S(2)}, u32[]{:S(2)}) collective-permute-start(bf16[128,512]{1,0:T(8,128)(2,1)} %bitcast.97), channel_id=1, source_target_pairs={{0,1},{1,2},{2,3},{3,4},{4,5},{5,6},{6,7},{7,0},{8,9},{9,10},{10,1... | collective-permute-start | bytes 393224 | tf_op jit(solution)/shard_map/ppermute | solution.py:37
  0.0 6.0 %collective-permute-start.1 = (bf16[128,512]{1,0:T(8,128)(2,1)}, bf16[128,512]{1,0:T(8,128)(2,1)S(1)}, u32[]{:S(2)}, u32[]{:S(2)}) collective-permute-start(bf16[128,512]{1,0:T(8,128)(2,1)} %bitcast.98), channel_id=1, source_target_pairs={{0,7},{1,0},{2,1},{3,2},{4,3},{5,4},{6,5},{7,6},{8,15},{9,8},{10,9... | collective-permute-start | bytes 393224 | tf_op jit(solution)/shard_map/ppermute | solution.py:42
  11.7 5.6 %collective-permute-start.4 = (bf16[128,512]{1,0:T(8,128)(2,1)S(1)}, bf16[128,512]{1,0:T(8,128)(2,1)S(1)}, u32[]{:S(2)}, u32[]{:S(2)}) collective-permute-start(bf16[128,512]{1,0:T(8,128)(2,1)S(1)} %collective-permute-done.2), channel_id=1, source_target_pairs={{0,1},{1,2},{2,3},{3,4},{4,5},{5,6},{6,7},{7,0},{8,9},{9,10},{10,1... | collective-permute-start | bytes 393224 | tf_op jit(solution)/shard_map/ppermute | solution.py:37
  17.4 5.6 %collective-permute-start.6 = (bf16[128,512]{1,0:T(8,128)(2,1)S(1)}, bf16[128,512]{1,0:T(8,128)(2,1)S(1)}, u32[]{:S(2)}, u32[]{:S(2)}) collective-permute-start(bf16[128,512]{1,0:T(8,128)(2,1)S(1)} %collective-permute-done.4), channel_id=1, source_target_pairs={{0,1},{1,2},{2,3},{3,4},{4,5},{5,6},{6,7},{7,0},{8,9},{9,10},{10,1... | collective-permute-start | bytes 393224 | tf_op jit(solution)/shard_map/ppermute | solution.py:37
  23.2 29.3 %collective-permute-start.8 = (bf16[1024,512]{0,1:T(8,128)(2,1)S(1)}, bf16[1024,512]{0,1:T(8,128)(2,1)S(1)}, u32[]{:S(2)}, u32[]{:S(2)}) collective-permute-start(bf16[1024,512]{0,1:T(8,128)(2,1)S(1)} %constant_dynamic-update-slice_fusion.40), channel_id=1, source_target_pairs={{8,0},{16,8},{24,16},{32,24},{40,32},{48,40},{56,48},{64,56},{72,6... | collective-permute-start | bytes 3145736 | tf_op jit(solution)/shard_map/ppermute | solution.py:10
  34.2 25.7 %collective-permute-start.7 = (bf16[1024,512]{0,1:T(8,128)(2,1)S(1)}, bf16[1024,512]{0,1:T(8,128)(2,1)S(1)}, u32[]{:S(2)}, u32[]{:S(2)}) collective-permute-start(bf16[1024,512]{0,1:T(8,128)(2,1)S(1)} %constant_dynamic-update-slice_fusion.40), channel_id=1, source_target_pairs={{0,8},{8,16},{16,24},{24,32},{32,40},{40,48},{48,56},{56,64},{64,7... | collective-permute-start | bytes 3145736 | tf_op jit(solution)/shard_map/ppermute | solution.py:10
  61.0 5.6 %collective-permute-start.9 = (bf16[128,512]{0,1:T(8,128)(2,1)S(1)}, bf16[128,512]{0,1:T(8,128)(2,1)S(1)}, u32[]{:S(2)}, u32[]{:S(2)}) collective-permute-start(bf16[128,512]{0,1:T(8,128)(2,1)S(1)} %get-tuple-element.6), channel_id=1, source_target_pairs={{0,1},{1,2},{2,3},{3,4},{4,5},{5,6},{6,7},{7,0},{8,9},{9,10},{10,1... | collective-permute-start | bytes 393224 | tf_op jit(solution)/shard_map/ppermute | solution.py:37
  61.1 5.6 %collective-permute-start.10 = (bf16[128,512]{0,1:T(8,128)(2,1)S(1)}, bf16[128,512]{0,1:T(8,128)(2,1)S(1)}, u32[]{:S(2)}, u32[]{:S(2)}) collective-permute-start(bf16[128,512]{0,1:T(8,128)(2,1)S(1)} %get-tuple-element.6), channel_id=1, source_target_pairs={{0,7},{1,0},{2,1},{3,2},{4,3},{5,4},{6,5},{7,6},{8,15},{9,8},{10,9... | collective-permute-start | bytes 393224 | tf_op jit(solution)/shard_map/ppermute | solution.py:42
  83.5 46.2 %collective-permute-start.17 = (bf16[1024,512]{0,1:T(8,128)(2,1)S(1)}, bf16[1024,512]{0,1:T(8,128)(2,1)S(1)}, u32[]{:S(2)}, u32[]{:S(2)}) collective-permute-start(bf16[1024,512]{0,1:T(8,128)(2,1)S(1)} %constant_dynamic-update-slice_fusion.32), channel_id=1, source_target_pairs={{16,0},{24,8},{32,16},{40,24},{48,32},{56,40},{64,48},{72,56},{80,... | collective-permute-start | bytes 3145736 | tf_op jit(solution)/shard_map/ppermute | solution.py:10
  85.4 48.8 %collective-permute-start.16 = (bf16[1024,512]{0,1:T(8,128)(2,1)S(1)}, bf16[1024,512]{0,1:T(8,128)(2,1)S(1)}, u32[]{:S(2)}, u32[]{:S(2)}) collective-permute-start(bf16[1024,512]{0,1:T(8,128)(2,1)S(1)} %constant_dynamic-update-slice_fusion.32), channel_id=1, source_target_pairs={{0,16},{8,24},{16,32},{24,40},{32,48},{40,56},{48,64},{56,72},{64,... | collective-permute-start | bytes 3145736 | tf_op jit(solution)/shard_map/ppermute | solution.py:10
  135.3 5.6 %collective-permute-start.18 = (bf16[128,512]{0,1:T(8,128)(2,1)S(1)}, bf16[128,512]{0,1:T(8,128)(2,1)S(1)}, u32[]{:S(2)}, u32[]{:S(2)}) collective-permute-start(bf16[128,512]{0,1:T(8,128)(2,1)S(1)} %get-tuple-element.8), channel_id=1, source_target_pairs={{0,1},{1,2},{2,3},{3,4},{4,5},{5,6},{6,7},{7,0},{8,9},{9,10},{10,1... | collective-permute-start | bytes 393224 | tf_op jit(solution)/shard_map/ppermute | solution.py:37
  135.4 5.6 %collective-permute-start.19 = (bf16[128,512]{0,1:T(8,128)(2,1)S(1)}, bf16[128,512]{0,1:T(8,128)(2,1)S(1)}, u32[]{:S(2)}, u32[]{:S(2)}) collective-permute-start(bf16[128,512]{0,1:T(8,128)(2,1)S(1)} %get-tuple-element.8), channel_id=1, source_target_pairs={{0,7},{1,0},{2,1},{3,2},{4,3},{5,4},{6,5},{7,6},{8,15},{9,8},{10,9... | collective-permute-start | bytes 393224 | tf_op jit(solution)/shard_map/ppermute | solution.py:42
  157.8 92.1 %collective-permute-start.26 = (bf16[1024,512]{0,1:T(8,128)(2,1)S(1)}, bf16[1024,512]{0,1:T(8,128)(2,1)S(1)}, u32[]{:S(2)}, u32[]{:S(2)}) collective-permute-start(bf16[1024,512]{0,1:T(8,128)(2,1)S(1)} %constant_dynamic-update-slice_fusion.24), channel_id=1, source_target_pairs={{32,0},{40,8},{48,16},{56,24},{64,32},{72,40},{80,48},{88,56},{96,... | collective-permute-start | bytes 3145736 | tf_op jit(solution)/shard_map/ppermute | solution.py:10
  159.7 90.7 %collective-permute-start.25 = (bf16[1024,512]{0,1:T(8,128)(2,1)S(1)}, bf16[1024,512]{0,1:T(8,128)(2,1)S(1)}, u32[]{:S(2)}, u32[]{:S(2)}) collective-permute-start(bf16[1024,512]{0,1:T(8,128)(2,1)S(1)} %constant_dynamic-update-slice_fusion.24), channel_id=1, source_target_pairs={{0,32},{8,40},{16,48},{24,56},{32,64},{40,72},{48,80},{56,88},{64,... | collective-permute-start | bytes 3145736 | tf_op jit(solution)/shard_map/ppermute | solution.py:10
  251.5 5.6 %collective-permute-start.28 = (bf16[128,512]{0,1:T(8,128)(2,1)S(1)}, bf16[128,512]{0,1:T(8,128)(2,1)S(1)}, u32[]{:S(2)}, u32[]{:S(2)}) collective-permute-start(bf16[128,512]{0,1:T(8,128)(2,1)S(1)} %get-tuple-element.10), channel_id=1, source_target_pairs={{0,7},{1,0},{2,1},{3,2},{4,3},{5,4},{6,5},{7,6},{8,15},{9,8},{10,9... | collective-permute-start | bytes 393224 | tf_op jit(solution)/shard_map/ppermute | solution.py:42
  273.9 22.7 %collective-permute-start.35 = (bf16[1024,512]{0,1:T(8,128)(2,1)S(1)}, bf16[1024,512]{0,1:T(8,128)(2,1)S(1)}, u32[]{:S(2)}, u32[]{:S(2)}) collective-permute-start(bf16[1024,512]{0,1:T(8,128)(2,1)S(1)} %constant_dynamic-update-slice_fusion.16), channel_id=1, source_target_pairs={{64,0},{72,8},{80,16},{88,24},{96,32},{104,40},{112,48},{120,56},{... | collective-permute-start | bytes 3145736 | tf_op jit(solution)/shard_map/ppermute | solution.py:10
  275.9 23.9 %collective-permute-start.34 = (bf16[1024,512]{0,1:T(8,128)(2,1)S(1)}, bf16[1024,512]{0,1:T(8,128)(2,1)S(1)}, u32[]{:S(2)}, u32[]{:S(2)}) collective-permute-start(bf16[1024,512]{0,1:T(8,128)(2,1)S(1)} %constant_dynamic-update-slice_fusion.16), channel_id=1, source_target_pairs={{0,64},{8,72},{16,80},{24,88},{32,96},{40,104},{48,112},{56,120},{... | collective-permute-start | bytes 3145736 | tf_op jit(solution)/shard_map/ppermute | solution.py:10
  300.9 5.6 %collective-permute-start.36 = (bf16[128,512]{0,1:T(8,128)(2,1)S(1)}, bf16[128,512]{0,1:T(8,128)(2,1)S(1)}, u32[]{:S(2)}, u32[]{:S(2)}) collective-permute-start(bf16[128,512]{0,1:T(8,128)(2,1)S(1)} %get-tuple-element.12), channel_id=1, source_target_pairs={{0,1},{1,2},{2,3},{3,4},{4,5},{5,6},{6,7},{7,0},{8,9},{9,10},{10,1... | collective-permute-start | bytes 393224 | tf_op jit(solution)/shard_map/ppermute | solution.py:37
  300.9 5.6 %collective-permute-start.37 = (bf16[128,512]{0,1:T(8,128)(2,1)S(1)}, bf16[128,512]{0,1:T(8,128)(2,1)S(1)}, u32[]{:S(2)}, u32[]{:S(2)}) collective-permute-start(bf16[128,512]{0,1:T(8,128)(2,1)S(1)} %get-tuple-element.12), channel_id=1, source_target_pairs={{0,7},{1,0},{2,1},{3,2},{4,3},{5,4},{6,5},{7,6},{8,15},{9,8},{10,9... | collective-permute-start | bytes 393224 | tf_op jit(solution)/shard_map/ppermute | solution.py:42
  323.3 46.0 %collective-permute-start.44 = (bf16[1024,512]{0,1:T(8,128)(2,1)S(1)}, bf16[1024,512]{0,1:T(8,128)(2,1)S(1)}, u32[]{:S(2)}, u32[]{:S(2)}) collective-permute-start(bf16[1024,512]{0,1:T(8,128)(2,1)S(1)} %constant_dynamic-update-slice_fusion.8), channel_id=1, source_target_pairs={{128,0},{136,8},{144,16},{152,24},{160,32},{168,40},{176,48},{184,... | collective-permute-start | bytes 3145736 | tf_op jit(solution)/shard_map/ppermute | solution.py:10
  325.3 47.2 %collective-permute-start.43 = (bf16[1024,512]{0,1:T(8,128)(2,1)S(1)}, bf16[1024,512]{0,1:T(8,128)(2,1)S(1)}, u32[]{:S(2)}, u32[]{:S(2)}) collective-permute-start(bf16[1024,512]{0,1:T(8,128)(2,1)S(1)} %constant_dynamic-update-slice_fusion.8), channel_id=1, source_target_pairs={{0,128},{8,136},{16,144},{24,152},{32,160},{40,168},{48,176},{56,1... | collective-permute-start | bytes 3145736 | tf_op jit(solution)/shard_map/ppermute | solution.py:10
  373.6 5.6 %collective-permute-start.46 = (bf16[128,512]{0,1:T(8,128)(2,1)S(1)}, bf16[128,512]{0,1:T(8,128)(2,1)S(1)}, u32[]{:S(2)}, u32[]{:S(2)}) collective-permute-start(bf16[128,512]{0,1:T(8,128)(2,1)S(1)} %get-tuple-element.14), channel_id=1, source_target_pairs={{0,7},{1,0},{2,1},{3,2},{4,3},{5,4},{6,5},{7,6},{8,15},{9,8},{10,9... | collective-permute-start | bytes 393224 | tf_op jit(solution)/shard_map/ppermute | solution.py:42
  396.0 20.4 %collective-permute-start.53 = (bf16[1024,512]{0,1:T(8,128)(2,1)S(1)}, bf16[1024,512]{0,1:T(8,128)(2,1)S(1)}, u32[]{:S(2)}, u32[]{:S(2)}) collective-permute-start(bf16[1024,512]{0,1:T(8,128)(2,1)S(1)} %constant_dynamic-update-slice_fusion), channel_id=1, source_target_pairs={{256,0},{264,8},{272,16},{280,24},{288,32},{296,40},{304,48},{312,... | collective-permute-start | bytes 3145736 | tf_op jit(solution)/shard_map/ppermute | solution.py:10
  397.4 49.0 %collective-permute-start.52 = (bf16[1024,512]{0,1:T(8,128)(2,1)S(1)}, bf16[1024,512]{0,1:T(8,128)(2,1)S(1)}, u32[]{:S(2)}, u32[]{:S(2)}) collective-permute-start(bf16[1024,512]{0,1:T(8,128)(2,1)S(1)} %constant_dynamic-update-slice_fusion), channel_id=1, source_target_pairs={{0,256},{8,264},{16,272},{24,280},{32,288},{40,296},{48,304},{56,3... | collective-permute-start | bytes 3145736 | tf_op jit(solution)/shard_map/ppermute | solution.py:10
  (33 other events, 258.9 us)
